TPU v7x, 32 devices: a whole 2x2x4 slice. The times are simulated.
32 devices in a mesh: row: 8 (over y, x, core), col: 4 (over z).
Axes of the slice: x: 2, y: 2, z: 4, core: 2. Of those that a mesh axis runs over, the one named last changes fastest.
Arguments:
- out_grads: bfloat16 [64, 28672], P('col', 'row'), may hold values from -6 to 6
- in_acts: bfloat16 [64, 8192], P('row', 'col'), may hold values from -6 to 6
- out_basis: bfloat16 [28672, 28672], P('row', 'col'), may hold values from -0.03125 to 0.03125
- in_basis: bfloat16 [8192, 8192], P('col', 'row'), may hold values from -0.0625 to 0.0625
- eigenvalues: bfloat16 [28672, 8192], P('col', 'row'), may hold values from 0.019897461 to 2
- queries: bfloat16 [2, 28672, 8192], P(None, 'col', 'row'), may hold values from -0.00015640259 to 0.00015640259
Outputs:
- scores: float32 [2, 64], replicated
All inputs are finite; a program needn't handle non-finite values.
Results may differ from a plain program's by a relative error of at most 0.0045.
Values may be sent and summed in bfloat16 or wider, within the bound.
No kernel may reach another device: no remote copies, remote signals or barrier semaphores. Data moves between devices by JAX's collectives and lax.ppermute only.
A program may use at most 192 MiB of HBM per device.

v0:
```python
import jax
import jax.numpy as jnp
from jax import lax
from jax.sharding import PartitionSpec as P

DAMPING = 0.1


def local(out_grads, in_acts, out_basis, in_basis, eigenvalues, queries):
    grads_all = lax.all_gather(out_grads, "col", axis=0, tiled=True)
    grad_mine = lax.psum_scatter(
        jnp.dot(grads_all, out_basis, preferred_element_type=jnp.float32),
        "row",
        scatter_dimension=0,
        tiled=True,
    ).astype(jnp.bfloat16)
    grad_rot = lax.all_gather(grad_mine, "row", axis=0, tiled=True)
    acts_all = lax.all_gather(in_acts, "row", axis=0, tiled=True)
    act_part = jnp.dot(acts_all, in_basis, preferred_element_type=jnp.float32)
    act_rot = lax.psum(act_part, "col").astype(jnp.bfloat16)
    shifted = eigenvalues.astype(jnp.float32) + DAMPING
    scaled = queries.astype(jnp.float32) / shifted[None]
    lifted = jnp.einsum(
        "qkj,tj->qkt",
        scaled,
        act_rot.astype(jnp.float32),
        precision=lax.Precision.HIGHEST,
        preferred_element_type=jnp.float32,
    )
    partial_scores = jnp.einsum(
        "qkt,tk->qt", lifted, grad_rot.astype(jnp.float32), precision=lax.Precision.HIGHEST
    )
    return lax.psum(partial_scores, ("row", "col"))


def solution(mesh):
    in_specs = (
        P("col", "row"),
        P("row", "col"),
        P("row", "col"),
        P("col", "row"),
        P("col", "row"),
        P(None, "col", "row"),
    )
    out_specs = P()
    return jax.shard_map(local, mesh=mesh, in_specs=in_specs, out_specs=out_specs, check_vma=False)
```

profile of v0, /device:TPU:0, one launch (start us, length us, event | category | flops | bytes accessed | tf_op | source)
XLA Modules:
  0.0 220.7 jit_solution(7782558009660924071)
XLA Ops:
  6.5 0.0 reduce-scatter.2.cloned.1.call-start
  6.5 17.0 %all_gather.9 = bf16[64,3584]{1,0:T(8,128)(2,1)S(1)} all-gather(bf16[16,3584]{1,0:T(8,128)(2,1)} %param.6), channel_id=1, replica_groups=mesh['row'=8,'col'=4] {'col'}, dimensions={0}, use_global_device_ids=true | all-gather | bytes 573440 | tf_op jit(solution)/shard_map/all_gather | solution.py:10
  23.5 21.8 %fusion.7 = f32[64,7168]{1,0:T(8,128)} fusion(bf16[64,3584]{1,0:T(8,128)(2,1)S(1)} %all_gather.9, bf16[3584,7168]{1,0:T(8,128)(2,1)} %param.8), kind=kOutput, calls=%fused_computation.9 | convolution fusion | flops 3288334336 | bytes 53673984 | tf_op jit(solution)/shard_map/dot_general | solution.py:12
  45.3 0.0 copy-start.1
  45.3 0.0 reduce-scatter.2.cloned.1.call-update
  45.4 0.0 copy-start
  45.4 17.4 %convert_add_fusion = f32[7168,1024]{1,0:T(8,128)} fusion(bf16[7168,1024]{1,0:T(8,128)(2,1)} %param.10), kind=kLoop, calls=%fused_computation.3 | loop fusion | flops 14680064 | bytes 44040192 | tf_op jit(solution)/shard_map/add | solution.py:21
  62.8 0.0 copy-done.1
  62.8 9.4 %all_gather.11 = bf16[64,2048]{1,0:T(8,128)(2,1)S(1)} all-gather(bf16[8,2048]{1,0:T(8,128)(2,1)S(1)} %copy-done.1), channel_id=1, replica_groups=mesh['row'=8,'col'=4] {'row'}, dimensions={0}, use_global_device_ids=true | all-gather | bytes 294912 | tf_op jit(solution)/shard_map/all_gather | solution.py:18
  72.2 0.0 copy-done
  72.2 0.8 fusion.8
  73.1 25.6 %all-reduce.1 = bf16[64,1024]{1,0:T(8,128)(2,1)S(1)} all-reduce(f32[64,1024]{1,0:T(8,128)S(1)} %fusion.8), channel_id=1, replica_groups=mesh['row'=8,'col'=4] {'col'}, use_global_device_ids=true, to_apply=%region_1.0 | all-reduce | flops 65536 | bytes 393216 | tf_op jit(solution)/shard_map/psum | solution.py:20
  98.7 45.4 %fusion = f32[2,7168,64]{1,2,0:T(8,128)} fusion(bf16[2,7168,1024]{2,1,0:T(8,128)(2,1)} %param.11, f32[7168,1024]{1,0:T(8,128)} %convert_add_fusion, bf16[64,1024]{1,0:T(8,128)(2,1)S(1)} %all-reduce.1), kind=kOutput, calls=%fused_computation.1 | convolution fusion | flops 11303649280 | bytes 62521344 | tf_op jit(solution)/shard_map/qkj,tj->qkt/dot_general | solution.py:23
  144.1 0.0 reduce-scatter.2.cloned.1.call-done
  144.1 1.0 convert_element_type.14
  145.1 11.0 %all_gather.10 = bf16[64,7168]{1,0:T(8,128)(2,1)S(1)} all-gather(bf16[8,7168]{1,0:T(8,128)(2,1)S(1)} %convert_element_type.14), channel_id=1, replica_groups=mesh['row'=8,'col'=4] {'row'}, dimensions={0}, use_global_device_ids=true | all-gather | bytes 1032192 | tf_op jit(solution)/shard_map/all_gather | solution.py:17
  156.0 19.9 %fusion.2 = f32[64,1,2]{2,1,0:T(1,128)S(1)} fusion(f32[2,7168,64]{1,2,0:T(8,128)} %fusion, bf16[64,7168,1]{1,0,2:T(8,128)(2,1)S(1)} %bitcast.11), kind=kOutput, calls=%fused_computation.4 | convolution fusion | flops 11010048 | bytes 4588032 | tf_op jit(solution)/shard_map/qkt,tk->qt/dot_general | solution.py:30
  175.9 0.1 copy.9
  176.0 37.8 %psum.15 = f32[2,64]{1,0:T(2,128)} all-reduce(f32[2,64]{1,0:T(2,128)S(1)} %bitcast.12), channel_id=1, replica_groups=mesh['row'=8,'col'=4] {'row','col'}, use_global_device_ids=true, to_apply=%region_2.0 | all-reduce | flops 128 | bytes 1024 | tf_op jit(solution)/shard_map/psum | solution.py:33
Async XLA Ops:
  6.5 137.6 %reduce-scatter.2.cloned.1.call-start = ((), (), s32[]{:S(2)}) async-start(), calls=%async_computation.1 | async-start | bytes 2064384 | tf_op jit(solution)/shard_map/reduce_scatter | solution.py:11
  45.3 17.4 %copy-start.1 = (bf16[8,2048]{1,0:T(8,128)(2,1)S(1)}, bf16[8,2048]{1,0:T(8,128)(2,1)}, u32[]{:S(2)}) copy-start(bf16[8,2048]{1,0:T(8,128)(2,1)} %param.7) | copy-start | bytes 98308
  45.4 26.8 %copy-start = (bf16[2048,1024]{1,0:T(8,128)(2,1)S(1)}, bf16[2048,1024]{1,0:T(8,128)(2,1)}, u32[]{:S(2)}) copy-start(bf16[2048,1024]{1,0:T(8,128)(2,1)} %param.9) | copy-start | bytes 12582916
Sparse Core Ops, SparseCore 0:
  45.5 42.0 reduce-scatter.1
where the time goes:
time: 221 us
  blocking collectives  101 us (46%)
  matrix products  88 us (40%)
  other arithmetic  18.3 us (8%)
  between operations  13.4 us (6%)
    dot_general x1, matrix products, local(): jnp.einsum('qkj,tj->qkt', scaled, act_rot.astype(jnp.float32), precision=...  45.4 us
    psum x1, blocking collectives, local(): return lax.psum(partial_scores, ('row', 'col'))  37.8 us
    psum x1, blocking collectives, local(): act_rot = lax.psum(act_part, 'col').astype(jnp.bfloat16)  25.6 us
    dot_general x1, matrix products, local(): jnp.dot(grads_all, out_basis, preferred_element_type=jnp.float32)  21.8 us
    dot_general x1, matrix products, local(): jnp.einsum('qkt,tk->qt', lifted, grad_rot.astype(jnp.float32), precision=...  19.9 us
    add x1, other arithmetic, local(): shifted = eigenvalues.astype(jnp.float32) + DAMPING  17.4 us
    all_gather x1, blocking collectives, local(): grads_all = lax.all_gather(out_grads, 'col', axis=0, tiled=True)  17 us
    all_gather x1, blocking collectives, local(): grad_rot = lax.all_gather(grad_mine, 'row', axis=0, tiled=True)  11 us
  transfers between devices with their start and end apart: 1, of which 0 were waited for; matrix products, arithmetic and copies ran while one was open for 29% of the time, Pallas kernels for 0%

commit v1 on v0

--- a/solution.py
+++ b/solution.py
@@ -30,7 +30,7 @@
     partial_scores = jnp.einsum(
         "qkt,tk->qt", lifted, grad_rot.astype(jnp.float32), precision=lax.Precision.HIGHEST
     )
-    return lax.psum(partial_scores, ("row", "col"))
+    return lax.psum(lax.psum(partial_scores, "col"), "row")
 
 
 def solution(mesh):

time: 221 us -> 204 us (0.923)
  blocking collectives: 101 us -> 83.7 us
    psum x1 -> x2, blocking collectives: 37.8 us -> 20.7 us  [local(): return lax.psum(lax.psum(partial_scores, 'col'), 'row')]
  transfers between devices with their start and end apart: 1 -> 1, of which waited for: 0 -> 0; matrix products, arithmetic and copies ran while one was open for 29% -> 31% of each run, Pallas kernels for 0% -> 0%
where the time goes in v1:
time: 204 us
  matrix products  88 us (43%)
  blocking collectives  83.7 us (41%)
  other arithmetic  18.3 us (9%)
  between operations  13.4 us (7%)
    dot_general x1, matrix products, local(): jnp.einsum('qkj,tj->qkt', scaled, act_rot.astype(jnp.float32), precision=...  45.4 us
    psum x1, blocking collectives, local(): act_rot = lax.psum(act_part, 'col').astype(jnp.bfloat16)  25.6 us
    dot_general x1, matrix products, local(): jnp.dot(grads_all, out_basis, preferred_element_type=jnp.float32)  21.8 us
    psum x2, blocking collectives, local(): return lax.psum(lax.psum(partial_scores, 'col'), 'row')  20.7 us
    dot_general x1, matrix products, local(): jnp.einsum('qkt,tk->qt', lifted, grad_rot.astype(jnp.float32), precision=...  19.9 us
    add x1, other arithmetic, local(): shifted = eigenvalues.astype(jnp.float32) + DAMPING  17.4 us
    all_gather x1, blocking collectives, local(): grads_all = lax.all_gather(out_grads, 'col', axis=0, tiled=True)  17 us
    all_gather x1, blocking collectives, local(): grad_rot = lax.all_gather(grad_mine, 'row', axis=0, tiled=True)  11 us
  transfers between devices with their start and end apart: 1, of which 0 were waited for; matrix products, arithmetic and copies ran while one was open for 31% of the time, Pallas kernels for 0%

profile of v1, /device:TPU:0, one launch (start us, length us, event | category | flops | bytes accessed | tf_op | source)
XLA Modules:
  0.0 203.6 jit_solution(13734869235012368840)
XLA Ops:
  6.5 0.0 reduce-scatter.2.cloned.1.call-start
  6.5 17.0 %all_gather.9 = bf16[64,3584]{1,0:T(8,128)(2,1)S(1)} all-gather(bf16[16,3584]{1,0:T(8,128)(2,1)} %param.6), channel_id=1, replica_groups=mesh['row'=8,'col'=4] {'col'}, dimensions={0}, use_global_device_ids=true | all-gather | bytes 573440 | tf_op jit(solution)/shard_map/all_gather | solution.py:10
  23.5 21.8 %fusion.7 = f32[64,7168]{1,0:T(8,128)} fusion(bf16[64,3584]{1,0:T(8,128)(2,1)S(1)} %all_gather.9, bf16[3584,7168]{1,0:T(8,128)(2,1)} %param.8), kind=kOutput, calls=%fused_computation.9 | convolution fusion | flops 3288334336 | bytes 53673984 | tf_op jit(solution)/shard_map/dot_general | solution.py:12
  45.3 0.0 copy-start.1
  45.3 0.0 reduce-scatter.2.cloned.1.call-update
  45.4 0.0 copy-start
  45.4 17.4 %convert_add_fusion = f32[7168,1024]{1,0:T(8,128)} fusion(bf16[7168,1024]{1,0:T(8,128)(2,1)} %param.10), kind=kLoop, calls=%fused_computation.3 | loop fusion | flops 14680064 | bytes 44040192 | tf_op jit(solution)/shard_map/add | solution.py:21
  62.8 0.0 copy-done.1
  62.8 9.4 %all_gather.11 = bf16[64,2048]{1,0:T(8,128)(2,1)S(1)} all-gather(bf16[8,2048]{1,0:T(8,128)(2,1)S(1)} %copy-done.1), channel_id=1, replica_groups=mesh['row'=8,'col'=4] {'row'}, dimensions={0}, use_global_device_ids=true | all-gather | bytes 294912 | tf_op jit(solution)/shard_map/all_gather | solution.py:18
  72.2 0.0 copy-done
  72.2 0.8 fusion.8
  73.1 25.6 %all-reduce.1 = bf16[64,1024]{1,0:T(8,128)(2,1)S(1)} all-reduce(f32[64,1024]{1,0:T(8,128)S(1)} %fusion.8), channel_id=1, replica_groups=mesh['row'=8,'col'=4] {'col'}, use_global_device_ids=true, to_apply=%region_1.0 | all-reduce | flops 65536 | bytes 393216 | tf_op jit(solution)/shard_map/psum | solution.py:20
  98.7 45.4 %fusion = f32[2,7168,64]{1,2,0:T(8,128)} fusion(bf16[2,7168,1024]{2,1,0:T(8,128)(2,1)} %param.11, f32[7168,1024]{1,0:T(8,128)} %convert_add_fusion, bf16[64,1024]{1,0:T(8,128)(2,1)S(1)} %all-reduce.1), kind=kOutput, calls=%fused_computation.1 | convolution fusion | flops 11303649280 | bytes 62521344 | tf_op jit(solution)/shard_map/qkj,tj->qkt/dot_general | solution.py:23
  144.1 0.0 reduce-scatter.2.cloned.1.call-done
  144.1 1.0 convert_element_type.14
  145.1 11.0 %all_gather.10 = bf16[64,7168]{1,0:T(8,128)(2,1)S(1)} all-gather(bf16[8,7168]{1,0:T(8,128)(2,1)S(1)} %convert_element_type.14), channel_id=1, replica_groups=mesh['row'=8,'col'=4] {'row'}, dimensions={0}, use_global_device_ids=true | all-gather | bytes 1032192 | tf_op jit(solution)/shard_map/all_gather | solution.py:17
  156.0 19.9 %fusion.2 = f32[64,1,2]{2,1,0:T(1,128)S(1)} fusion(f32[2,7168,64]{1,2,0:T(8,128)} %fusion, bf16[64,7168,1]{1,0,2:T(8,128)(2,1)S(1)} %bitcast.11), kind=kOutput, calls=%fused_computation.4 | convolution fusion | flops 11010048 | bytes 4588032 | tf_op jit(solution)/shard_map/qkt,tk->qt/dot_general | solution.py:30
  175.9 0.1 copy.9
  176.0 8.4 %psum.22 = f32[2,64]{1,0:T(2,128)S(1)} all-reduce(f32[2,64]{1,0:T(2,128)S(1)} %bitcast.12), channel_id=1, replica_groups=mesh['row'=8,'col'=4] {'col'}, use_global_device_ids=true, to_apply=%region_2.0 | all-reduce | flops 128 | bytes 1024 | tf_op jit(solution)/shard_map/psum | solution.py:33
  184.4 12.3 %psum.23 = f32[2,64]{1,0:T(2,128)} all-reduce(f32[2,64]{1,0:T(2,128)S(1)} %psum.22), channel_id=1, replica_groups=mesh['row'=8,'col'=4] {'row'}, use_global_device_ids=true, to_apply=%region_3.0 | all-reduce | flops 128 | bytes 1024 | tf_op jit(solution)/shard_map/psum | solution.py:33
Async XLA Ops:
  6.5 137.6 %reduce-scatter.2.cloned.1.call-start = ((), (), s32[]{:S(2)}) async-start(), calls=%async_computation.1 | async-start | bytes 2064384 | tf_op jit(solution)/shard_map/reduce_scatter | solution.py:11
  45.3 17.4 %copy-start.1 = (bf16[8,2048]{1,0:T(8,128)(2,1)S(1)}, bf16[8,2048]{1,0:T(8,128)(2,1)}, u32[]{:S(2)}) copy-start(bf16[8,2048]{1,0:T(8,128)(2,1)} %param.7) | copy-start | bytes 98308
  45.4 26.8 %copy-start = (bf16[2048,1024]{1,0:T(8,128)(2,1)S(1)}, bf16[2048,1024]{1,0:T(8,128)(2,1)}, u32[]{:S(2)}) copy-start(bf16[2048,1024]{1,0:T(8,128)(2,1)} %param.9) | copy-start | bytes 12582916
Sparse Core Ops, SparseCore 0:
  45.5 42.0 reduce-scatter.1
